TPU v7x, 256 devices: a whole 4x4x8 slice. The times are simulated.
256 devices in a mesh: dp: 16 (over y_lo, x, core), tensor: 16 (over y_hi, z).
Axes of the slice: x: 4, y: 4 (y_hi: 2, y_lo: 2; y = y_hi * 2 + y_lo), z: 8, core: 2. Of those that a mesh axis runs over, the one named last changes fastest.
Arguments:
- tokens: bfloat16 [12288, 8192], P(('dp', 'tensor')), may hold values from -6 to 6
- q_weight: bfloat16 [8192, 8192], P(None, 'tensor'), may hold values from -0.0625 to 0.0625
- pool_down: bfloat16 [128, 64, 8192], P('dp', None, 'tensor'), may hold values from -0.0625 to 0.0625
- pool_up: bfloat16 [128, 64, 8192], P('dp', None, 'tensor'), may hold values from -0.75 to 0.75
- block_units: int32 [16, 8], replicated, may hold values from 1 to 24, 48 in all within a row
- adapter_ids: int32 [16, 8], replicated, may hold values from 0 to 127, as said below
- location: int32 [128], replicated, may hold values from 0 to 127, as said below
Outputs:
- queries: bfloat16 [12288, 8192], P('dp', 'tensor')
Inputs may be any that keep to these rules, and one draw needn't show every extreme that they name: `adapter_ids`: the 8 adapters of one group lie in pool rows of 8 different dp shards (row location[a] lies on shard location[a] // 8). A permutation: adapter a is held in pool row location[a]. `block_units`: each group's blocks sum to 48; the largest is exactly 24.
All inputs are finite; a program needn't handle non-finite values.
Results may differ from a plain program's by a relative error of at most 0.0029.
Values may be sent and summed in bfloat16 or wider, within the bound.
No kernel may reach another device: no remote copies, remote signals or barrier semaphores. Data moves between devices by JAX's collectives and lax.ppermute only.
A program may use at most 128 MiB of HBM per device.

v0:
```python
import jax
import jax.numpy as jnp
from jax import lax
from jax.sharding import PartitionSpec as P

adapter_scale = 0.5


def tenant_mask(pool_unit_row, group_rows, tenants):
    block_ends = 16 * jnp.cumsum(pool_unit_row)
    positions = jnp.arange(group_rows, dtype=jnp.int32)
    tenant_index = jnp.sum((positions[:, None] >= block_ends[None, :]).astype(jnp.int32), axis=1)
    return tenant_index[:, None] == jnp.arange(tenants, dtype=jnp.int32)[None, :]


def select_rows(one_hot, table):
    picked = jnp.einsum(
        "ks,srd->krd", one_hot.astype(jnp.bfloat16), table, preferred_element_type=jnp.float32
    )
    return picked.astype(jnp.bfloat16)


def on_device(tokens, q_weight, pool_down, pool_up, block_units, adapter_ids, location):
    my_group = lax.axis_index("dp")
    tenants = adapter_ids.shape[1]
    rank_size = pool_down.shape[1]
    local_width = pool_down.shape[2]
    columns = q_weight.shape[1]
    pool_total = location.shape[0]
    id_hits = adapter_ids[:, :, None] == jnp.arange(pool_total, dtype=jnp.int32)[None, None, :]
    slot_ids = jnp.sum(jnp.where(id_hits, location[None, None, :], 0), axis=2)
    my_slots = lax.dynamic_index_in_dim(slot_ids, my_group, 0, keepdims=False)
    whole_down, whole_up = (
        lax.all_gather(pool_down, "dp", axis=0, tiled=True),
        lax.all_gather(pool_up, "dp", axis=0, tiled=True),
    )
    pick_rows = my_slots[:, None] == jnp.arange(pool_total, dtype=jnp.int32)[None, :]
    panels_down = select_rows(pick_rows, whole_down)
    panels_up = select_rows(pick_rows, whole_up)
    down_flat = panels_down.reshape(tenants * rank_size, local_width)
    up_flat = panels_up.reshape(tenants * rank_size, columns)
    width_start = lax.axis_index("tensor") * local_width
    row_block = lax.all_gather(tokens, "tensor", axis=0, tiled=True)
    base_projection = jnp.dot(row_block, q_weight, preferred_element_type=jnp.float32)
    local_cols = lax.dynamic_slice_in_dim(row_block, width_start, local_width, 1)
    wide_part = lax.dot_general(
        local_cols, down_flat, (((1,), (1,)), ((), ())), preferred_element_type=jnp.float32
    )
    combined = jnp.concatenate([base_projection, wide_part], axis=1)
    group_rows = combined.shape[0]
    base_projection = combined[:, :columns]
    wide_part = combined[:, columns:].reshape(group_rows, tenants, rank_size)
    pool_unit_row = lax.dynamic_index_in_dim(block_units, my_group, 0, keepdims=False)
    tenant_masks = tenant_mask(pool_unit_row, group_rows, tenants)
    partial_low = jnp.sum(
        jnp.where(tenant_masks[:, :, None], wide_part, jnp.zeros((), jnp.float32)), axis=1
    )
    packed = partial_low.reshape(group_rows * rank_size // 128, 128)
    low_rank = lax.psum(packed, "tensor").astype(jnp.bfloat16)
    low_rank = low_rank.reshape(group_rows, rank_size)
    low_wide = jnp.where(
        tenant_masks[:, :, None], low_rank[:, None, :], jnp.zeros((), jnp.bfloat16)
    )
    adapter_contribution = jnp.dot(
        low_wide.reshape(group_rows, tenants * rank_size),
        up_flat,
        preferred_element_type=jnp.float32,
    )
    return (base_projection + adapter_scale * adapter_contribution).astype(jnp.bfloat16)


def solution(mesh):
    placed = (
        P(("dp", "tensor"), None),
        P(None, "tensor"),
        P("dp", None, "tensor"),
        P("dp", None, "tensor"),
        P(),
        P(),
        P(),
    )
    return jax.shard_map(
        on_device, mesh=mesh, in_specs=placed, out_specs=P("dp", "tensor"), check_vma=False
    )
```

profile of v0, /device:TPU:2, one launch (start us, length us, event | category | flops | bytes accessed | tf_op | source)
XLA Modules:
  0.0 403.1 jit_solution(1845596998475962294)
XLA Ops:
  6.5 0.0 copy-start
  6.5 0.7 all-gather.6.cloned.1.call-update
  7.3 0.0 all-gather.8.cloned.1.call-start
  7.3 0.7 all-gather.8.cloned.1.call-update
  8.0 0.0 all-gather.4.cloned.1.call-start
  8.1 0.7 all-gather.4.cloned.1.call-update
  8.7 0.8 copy.18
  9.5 0.2 dynamic-slice_reduce_fusion
  9.7 0.2 reduce-window.8
  9.9 1.1 select_reduce_fusion.1
  11.0 0.1 convert_reduce_fusion
  11.1 55.6 %all-gather.6.cloned.1.call-done = bf16[128,64,512]{2,1,0:T(8,128)(2,1)} async-done(((bf16[8,64,512]{2,1,0:T(8,128)(2,1)}), bf16[128,64,512]{2,1,0:T(8,128)(2,1)}) %all-gather.6.cloned.1.call-update) | async-done | bytes 8388624 | tf_op jit(solution)/shard_map/all_gather | solution.py:34
  66.7 12.2 %fusion.6 = bf16[8,64,512]{2,0,1:T(8,128)(2,1)S(1)} fusion(bf16[128,64,512]{2,1,0:T(8,128)(2,1)} %all-gather.6.cloned.1.call-done, s32[8]{0:T(128)S(1)} %fusion.27), kind=kOutput, calls=%fused_computation.8 | convolution fusion | flops 67372032 | bytes 8912928 | tf_op jit(solution)/shard_map/ks,srd->krd/dot_general | solution.py:17
  78.8 45.2 %all-gather.8.cloned.1.call-done = bf16[128,64,512]{2,1,0:T(8,128)(2,1)} async-done(((bf16[8,64,512]{2,1,0:T(8,128)(2,1)}), bf16[128,64,512]{2,1,0:T(8,128)(2,1)}) %all-gather.8.cloned.1.call-update) | async-done | bytes 8388624 | tf_op jit(solution)/shard_map/all_gather | solution.py:35
  124.0 12.3 %fusion.9 = bf16[8,64,512]{2,0,1:T(8,128)(2,1)S(1)} fusion(bf16[128,64,512]{2,1,0:T(8,128)(2,1)} %all-gather.8.cloned.1.call-done, s32[8]{0:T(128)S(1)} %fusion.27), kind=kOutput, calls=%fused_computation.9 | convolution fusion | flops 67372032 | bytes 8912928 | tf_op jit(solution)/shard_map/ks,srd->krd/dot_general | solution.py:17
  136.4 169.6 %all-gather.4.cloned.1.call-done = bf16[768,8192]{1,0:T(8,128)(2,1)} async-done(((bf16[48,8192]{1,0:T(8,128)(2,1)}), bf16[768,8192]{1,0:T(8,128)(2,1)}) %all-gather.4.cloned.1.call-update) | async-done | bytes 12582928 | tf_op jit(solution)/shard_map/all_gather | solution.py:43
  306.0 1.8 select_reduce_fusion
  307.8 0.2 copy.21
  308.0 0.1 reshape.63
  308.1 74.8 %all-reduce.1 = bf16[384,128]{1,0:T(8,128)(2,1)S(1)} all-reduce(f32[384,128]{1,0:T(8,128)S(1)} %reshape.63), channel_id=1, replica_groups=mesh['dp'=16,'tensor'=16] {'tensor'}, use_global_device_ids=true, to_apply=%region_4.5 | all-reduce | flops 49152 | bytes 294912 | tf_op jit(solution)/shard_map/psum | solution.py:59
  382.9 0.1 broadcast_in_dim.59
  383.0 0.1 copy.22
  383.1 0.6 fusion.13
  383.8 12.8 %fusion.5 = bf16[768,512]{1,0:T(8,128)(2,1)} fusion(f32[768,512,1]{1,0,2:T(8,128)S(1)} %fusion.13, bf16[768,8192]{1,0:T(8,128)(2,1)} %all-gather.4.cloned.1.call-done, bf16[8192,512]{1,0:T(8,128)(2,1)} %param.8), kind=kOutput, calls=%fused_computation.6 | convolution fusion | flops 6443630592 | bytes 23330816 | tf_op jit(solution)/shard_map/dot_general | solution.py:44
  (5 shorter events, 0.0 us)
Async XLA Ops:
  6.5 3.0 copy-start
  6.5 60.1 %all-gather.6.cloned.1.call-start = ((), (), s32[]{:S(2)}) async-start(), calls=%async_computation.1 | async-start | bytes 8912896 | tf_op jit(solution)/shard_map/all_gather | solution.py:34
  7.3 116.8 %all-gather.8.cloned.1.call-start = ((), (), s32[]{:S(2)}) async-start(), calls=%async_computation.2 | async-start | bytes 8912896 | tf_op jit(solution)/shard_map/all_gather | solution.py:35
  8.0 298.0 %all-gather.4.cloned.1.call-start = ((), (), s32[]{:S(2)}) async-start(), calls=%async_computation | async-start | bytes 13369344 | tf_op jit(solution)/shard_map/all_gather | solution.py:43
Sparse Core Ops, SparseCore 0:
  9.2 57.4 all-gather.5
  68.5 55.4 all-gather.7
  126.6 179.3 all-gather.3
where the time goes:
time: 403 us
  waiting for transfers between devices  272 us (67%)
  blocking collectives  74.8 us (19%)
  matrix products  39.7 us (10%)
  between operations  13.2 us (3%)
    all_gather x1, waiting for transfers between devices, on_device(): row_block = lax.all_gather(tokens, 'tensor', axis=0, tiled=True)  170 us
    psum x1, blocking collectives, on_device(): low_rank = lax.psum(packed, 'tensor').astype(jnp.bfloat16)  74.8 us
    all_gather x1, waiting for transfers between devices, on_device(): lax.all_gather(pool_down, 'dp', axis=0, tiled=True)  55.6 us
    all_gather x1, waiting for transfers between devices, on_device(): lax.all_gather(pool_up, 'dp', axis=0, tiled=True)  45.2 us
    dot_general x2, matrix products, select_rows(): jnp.einsum('ks,srd->krd', one_hot.astype(jnp.bfloat16), table, preferred_...  24.5 us
    dot_general x1, matrix products, on_device(): jnp.dot(row_block, q_weight, preferred_element_type=jnp.float32)  12.8 us
  transfers between devices with their start and end apart: 3, of which 3 were waited for; matrix products, arithmetic and copies ran while one was open for 7% of the time, Pallas kernels for 0%

commit v1 on v0

--- a/solution.py
+++ b/solution.py
@@ -40,7 +40,9 @@
     down_flat = panels_down.reshape(tenants * rank_size, local_width)
     up_flat = panels_up.reshape(tenants * rank_size, columns)
     width_start = lax.axis_index("tensor") * local_width
-    row_block = lax.all_gather(tokens, "tensor", axis=0, tiled=True)
+    row_block = jnp.concatenate(
+        lax.all_to_all(jnp.stack([tokens] * lax.axis_size("tensor")), "tensor", 0, 0), axis=0
+    )
     base_projection = jnp.dot(row_block, q_weight, preferred_element_type=jnp.float32)
     local_cols = lax.dynamic_slice_in_dim(row_block, width_start, local_width, 1)
     wide_part = lax.dot_general(

time: 403 us -> 413 us (1.025)
  waiting for transfers between devices: 272 us -> 255 us
  starting transfers between devices: 0.08 us -> 11.4 us
  blocking collectives: 74.8 us -> 83.4 us
  local copies, waits for them, and re-layouts: 1.49 us -> 7.97 us
    all_gather x1 -> x0, waiting for transfers between devices: 170 us -> none  [on_device(): row_block = lax.all_gather(tokens, 'tensor', axis=0, tiled=True)]
    all_gather x1, waiting for transfers between devices: 45.2 us -> 110 us  [on_device(): lax.all_gather(pool_up, 'dp', axis=0, tiled=True)]
    all_to_all x0 -> x1, waiting for transfers between devices: none -> 54.8 us  [on_device(): lax.all_to_all(jnp.stack([tokens] * lax.axis_size('tensor')), 'tensor', 0...]
    all_gather x1, waiting for transfers between devices: 55.6 us -> 88.4 us  [on_device(): lax.all_gather(pool_down, 'dp', axis=0, tiled=True)]
    all_to_all x0 -> x1, starting transfers between devices: none -> 11.4 us  [on_device(): lax.all_to_all(jnp.stack([tokens] * lax.axis_size('tensor')), 'tensor', 0...]
    psum x1, blocking collectives: 74.8 us -> 83.4 us  [on_device(): low_rank = lax.psum(packed, 'tensor').astype(jnp.bfloat16)]
    another operation x0 -> x1, local copies, waits for them, and re-layouts: none -> 7.16 us  [on_device(): jnp.stack([tokens] * lax.axis_size('tensor'))]
  transfers between devices with their start and end apart: 3 -> 3, of which waited for: 3 -> 3; matrix products, arithmetic and copies ran while one was open for 7% -> 8% of each run, Pallas kernels for 0% -> 0%
where the time goes in v1:
time: 413 us; the launch traced here: 411 us
  waiting for transfers between devices  255 us (62%)
  blocking collectives  83.4 us (20%)
  matrix products  39.7 us (10%)
  between operations  13.5 us (3%)
  starting transfers between devices  11.4 us (3%)
  local copies, waits for them, and re-layouts  7.97 us (2%)
    all_gather x1, waiting for transfers between devices, on_device(): lax.all_gather(pool_up, 'dp', axis=0, tiled=True)  110 us
    all_gather x1, waiting for transfers between devices, on_device(): lax.all_gather(pool_down, 'dp', axis=0, tiled=True)  88.4 us
    psum x1, blocking collectives, on_device(): low_rank = lax.psum(packed, 'tensor').astype(jnp.bfloat16)  83.4 us
    all_to_all x1, waiting for transfers between devices, on_device(): lax.all_to_all(jnp.stack([tokens] * lax.axis_size('tensor')), 'tensor', 0...  54.8 us
    dot_general x2, matrix products, select_rows(): jnp.einsum('ks,srd->krd', one_hot.astype(jnp.bfloat16), table, preferred_...  24.5 us
    dot_general x1, matrix products, on_device(): jnp.dot(row_block, q_weight, preferred_element_type=jnp.float32)  12.8 us
    all_to_all x1, starting transfers between devices, on_device(): lax.all_to_all(jnp.stack([tokens] * lax.axis_size('tensor')), 'tensor', 0...  11.4 us
  transfers between devices with their start and end apart: 3, of which 3 were waited for; matrix products, arithmetic and copies ran while one was open for 8% of the time, Pallas kernels for 0%

profile of v1, /device:TPU:2, one launch (start us, length us, event | category | flops | bytes accessed | tf_op | source)
XLA Modules:
  0.0 411.5 jit_solution(17513035172935970253)
XLA Ops:
  6.5 0.0 copy-start
  6.5 0.7 all-gather.3.cloned.1.call-update
  7.3 7.2 %stack.2 = bf16[16,48,8192]{2,1,0:T(8,128)(2,1)} broadcast(bf16[48,8192]{1,0:T(8,128)(2,1)} %param.7), dimensions={1,2} | broadcast | bytes 13369344 | tf_op jit(solution)/shard_map/stack | solution.py:44
  14.4 11.4 %all-to-all-start = ((bf16[16,48,8192]{2,1,0:T(8,128)(2,1)}), bf16[16,48,8192]{2,1,0:T(8,128)(2,1)}, u32[]{:S(2)}, u32[]{:S(2)}) async-start(bf16[16,48,8192]{2,1,0:T(8,128)(2,1)} %stack.2), calls=%async_computation | async-start | bytes 25165824 | tf_op jit(solution)/shard_map/all_to_all | solution.py:44
  25.8 0.0 all-gather.5.cloned.1.call-start
  25.9 0.7 all-gather.5.cloned.1.call-update
  26.6 0.1 copy.18
  26.6 0.2 dynamic-slice_reduce_fusion
  26.8 0.2 reduce-window.8
  27.0 0.4 select_reduce_fusion.1
  27.5 0.1 convert_reduce_fusion
  27.6 88.4 %all-gather.3.cloned.1.call-done = bf16[128,64,512]{2,1,0:T(8,128)(2,1)} async-done(((bf16[8,64,512]{2,1,0:T(8,128)(2,1)}), bf16[128,64,512]{2,1,0:T(8,128)(2,1)}) %all-gather.3.cloned.1.call-update) | async-done | bytes 8388624 | tf_op jit(solution)/shard_map/all_gather | solution.py:34
  115.9 12.2 %fusion.6 = bf16[8,64,512]{2,0,1:T(8,128)(2,1)S(1)} fusion(bf16[128,64,512]{2,1,0:T(8,128)(2,1)} %all-gather.3.cloned.1.call-done, s32[8]{0:T(128)S(1)} %fusion.27), kind=kOutput, calls=%fused_computation.8 | convolution fusion | flops 67372032 | bytes 8912928 | tf_op jit(solution)/shard_map/ks,srd->krd/dot_general | solution.py:17
  128.1 110.2 %all-gather.5.cloned.1.call-done = bf16[128,64,512]{2,1,0:T(8,128)(2,1)} async-done(((bf16[8,64,512]{2,1,0:T(8,128)(2,1)}), bf16[128,64,512]{2,1,0:T(8,128)(2,1)}) %all-gather.5.cloned.1.call-update) | async-done | bytes 8388624 | tf_op jit(solution)/shard_map/all_gather | solution.py:35
  238.3 12.3 %fusion.9 = bf16[8,64,512]{2,0,1:T(8,128)(2,1)S(1)} fusion(bf16[128,64,512]{2,1,0:T(8,128)(2,1)} %all-gather.5.cloned.1.call-done, s32[8]{0:T(128)S(1)} %fusion.27), kind=kOutput, calls=%fused_computation.9 | convolution fusion | flops 67372032 | bytes 8912928 | tf_op jit(solution)/shard_map/ks,srd->krd/dot_general | solution.py:17
  250.6 54.8 %all-to-all-done = bf16[16,48,8192]{2,1,0:T(8,128)(2,1)} async-done(((bf16[16,48,8192]{2,1,0:T(8,128)(2,1)}), bf16[16,48,8192]{2,1,0:T(8,128)(2,1)}, u32[]{:S(2)}, u32[]{:S(2)}) %all-to-all-start) | async-done | bytes 12582944 | tf_op jit(solution)/shard_map/all_to_all | solution.py:44
  305.4 1.8 select_reduce_fusion
  307.2 0.2 copy.21
  307.4 0.1 reshape.69
  307.5 83.4 %all-reduce.1 = bf16[384,128]{1,0:T(8,128)(2,1)S(1)} all-reduce(f32[384,128]{1,0:T(8,128)S(1)} %reshape.69), channel_id=1, replica_groups=mesh['dp'=16,'tensor'=16] {'tensor'}, use_global_device_ids=true, to_apply=%region_4.5 | all-reduce | flops 49152 | bytes 294912 | tf_op jit(solution)/shard_map/psum | solution.py:61
  390.9 0.1 broadcast_in_dim.59
  391.1 0.1 copy.22
  391.2 0.6 fusion.13
  391.8 12.8 %fusion.5 = bf16[768,512]{1,0:T(8,128)(2,1)} fusion(f32[768,512,1]{1,0,2:T(8,128)S(1)} %fusion.13, bf16[768,8192]{1,0:T(8,128)(2,1)} %bitcast, bf16[8192,512]{1,0:T(8,128)(2,1)} %param.8), kind=kOutput, calls=%fused_computation.6 | convolution fusion | flops 6443630592 | bytes 23330816 | tf_op jit(solution)/shard_map/dot_general | solution.py:46
  (9 shorter events, 0.0 us)
Async XLA Ops:
  6.5 20.1 %copy-start = (s32[16,8]{0,1:T(8,128)S(1)}, s32[16,8]{0,1:T(8,128)}, u32[]{:S(2)}) copy-start(s32[16,8]{0,1:T(8,128)} %param.11) | copy-start | bytes 1540
  6.5 109.4 %all-gather.3.cloned.1.call-start = ((), (), s32[]{:S(2)}) async-start(), calls=%async_computation.1 | async-start | bytes 8912896 | tf_op jit(solution)/shard_map/all_gather | solution.py:34
  14.4 12.1 %copy-start.1 = (s32[16,8]{0,1:T(8,128)S(1)}, s32[16,8]{0,1:T(8,128)}, u32[]{:S(2)}) copy-start(s32[16,8]{0,1:T(8,128)} %param.12) | copy-start | bytes 1540
  14.4 12.6 %copy-start.2 = (s32[128]{0:T(128)S(1)}, s32[128]{0:T(128)}, u32[]{:S(2)}) copy-start(s32[128]{0:T(128)} %param.13) | copy-start | bytes 1540
  14.4 291.0 %all-to-all-start = ((bf16[16,48,8192]{2,1,0:T(8,128)(2,1)}), bf16[16,48,8192]{2,1,0:T(8,128)(2,1)}, u32[]{:S(2)}, u32[]{:S(2)}) async-start(bf16[16,48,8192]{2,1,0:T(8,128)(2,1)} %stack.2), calls=%async_computation | async-start | bytes 25165824 | tf_op jit(solution)/shard_map/all_to_all | solution.py:44
  25.8 212.5 %all-gather.5.cloned.1.call-start = ((), (), s32[]{:S(2)}) async-start(), calls=%async_computation.2 | async-start | bytes 8912896 | tf_op jit(solution)/shard_map/all_gather | solution.py:35
Sparse Core Ops, SparseCore 0:
  9.2 106.6 all-gather.2
  117.8 120.4 all-gather.4

commit v2 on v0

--- a/solution.py
+++ b/solution.py
@@ -56,7 +56,7 @@
         jnp.where(tenant_masks[:, :, None], wide_part, jnp.zeros((), jnp.float32)), axis=1
     )
     packed = partial_low.reshape(group_rows * rank_size // 128, 128)
-    low_rank = lax.psum(packed, "tensor").astype(jnp.bfloat16)
+    low_rank = jnp.sum(lax.all_gather(packed, "tensor"), axis=0).astype(jnp.bfloat16)
     low_rank = low_rank.reshape(group_rows, rank_size)
     low_wide = jnp.where(
         tenant_masks[:, :, None], low_rank[:, None, :], jnp.zeros((), jnp.bfloat16)

time: 403 us -> 420 us (1.042)
  waiting for transfers between devices: 272 us -> 361 us
  blocking collectives: 74.8 us -> 0 us
    all_gather x0 -> x1, waiting for transfers between devices: none -> 83.5 us  [on_device(): lax.all_gather(packed, 'tensor')]
    psum x1 -> x0, blocking collectives: 74.8 us -> none  [on_device(): low_rank = lax.psum(packed, 'tensor').astype(jnp.bfloat16)]
    all_gather x1, waiting for transfers between devices: 45.2 us -> 50.4 us  [on_device(): lax.all_gather(pool_up, 'dp', axis=0, tiled=True)]
  transfers between devices with their start and end apart: 3 -> 4, of which waited for: 3 -> 4; matrix products, arithmetic and copies ran while one was open for 7% -> 7% of each run, Pallas kernels for 0% -> 0%
where the time goes in v2:
time: 420 us
  waiting for transfers between devices  361 us (86%)
  matrix products  39.7 us (9%)
  between operations  13.2 us (3%)
    all_gather x1, waiting for transfers between devices, on_device(): row_block = lax.all_gather(tokens, 'tensor', axis=0, tiled=True)  170 us
    all_gather x1, waiting for transfers between devices, on_device(): lax.all_gather(packed, 'tensor')  83.5 us
    all_gather x1, waiting for transfers between devices, on_device(): lax.all_gather(pool_down, 'dp', axis=0, tiled=True)  55.5 us
    all_gather x1, waiting for transfers between devices, on_device(): lax.all_gather(pool_up, 'dp', axis=0, tiled=True)  50.4 us
    dot_general x2, matrix products, select_rows(): jnp.einsum('ks,srd->krd', one_hot.astype(jnp.bfloat16), table, preferred_...  24.5 us
    dot_general x1, matrix products, on_device(): jnp.dot(row_block, q_weight, preferred_element_type=jnp.float32)  12.8 us
  transfers between devices with their start and end apart: 4, of which 4 were waited for; matrix products, arithmetic and copies ran while one was open for 7% of the time, Pallas kernels for 0%

profile of v2, /device:TPU:2, one launch (start us, length us, event | category | flops | bytes accessed | tf_op | source)
XLA Modules:
  0.0 419.9 jit_solution(1842811214956417207)
XLA Ops:
  6.5 0.7 all-gather.7.cloned.1.call-update
  7.3 0.0 all-gather.5.cloned.1.call-start
  7.3 0.7 all-gather.5.cloned.1.call-update
  8.1 0.7 all-gather.11.cloned.1.call-update
  8.7 0.0 all-gather.9.cloned.1.call-start
  8.8 0.8 copy.18
  9.6 0.2 dynamic-slice_reduce_fusion
  9.7 0.2 reduce-window.8
  9.9 1.1 select_reduce_fusion.1
  11.0 0.1 convert_reduce_fusion
  11.1 55.5 %all-gather.7.cloned.1.call-done = bf16[128,64,512]{2,1,0:T(8,128)(2,1)} async-done(((bf16[8,64,512]{2,1,0:T(8,128)(2,1)}), bf16[128,64,512]{2,1,0:T(8,128)(2,1)}) %all-gather.7.cloned.1.call-update) | async-done | bytes 8388624 | tf_op jit(solution)/shard_map/all_gather | solution.py:34
  66.7 12.2 %fusion.6 = bf16[8,64,512]{2,0,1:T(8,128)(2,1)S(1)} fusion(bf16[128,64,512]{2,1,0:T(8,128)(2,1)} %all-gather.7.cloned.1.call-done, s32[8]{0:T(128)S(1)} %fusion.27), kind=kOutput, calls=%fused_computation.8 | convolution fusion | flops 67372032 | bytes 8912928 | tf_op jit(solution)/shard_map/ks,srd->krd/dot_general | solution.py:17
  78.8 169.8 %all-gather.5.cloned.1.call-done = bf16[768,8192]{1,0:T(8,128)(2,1)} async-done(((bf16[48,8192]{1,0:T(8,128)(2,1)}), bf16[768,8192]{1,0:T(8,128)(2,1)}) %all-gather.5.cloned.1.call-update) | async-done | bytes 12582928 | tf_op jit(solution)/shard_map/all_gather | solution.py:43
  248.6 1.8 select_reduce_fusion
  250.4 0.2 copy.21
  250.6 0.8 all_gather_reshape.3
  251.4 50.4 %all-gather.11.cloned.1.call-done = bf16[128,64,512]{2,1,0:T(8,128)(2,1)} async-done(((bf16[8,64,512]{2,1,0:T(8,128)(2,1)}), bf16[128,64,512]{2,1,0:T(8,128)(2,1)}) %all-gather.11.cloned.1.call-update) | async-done | bytes 8388624 | tf_op jit(solution)/shard_map/all_gather | solution.py:35
  301.8 12.3 %fusion.9 = bf16[8,64,512]{2,0,1:T(8,128)(2,1)S(1)} fusion(bf16[128,64,512]{2,1,0:T(8,128)(2,1)} %all-gather.11.cloned.1.call-done, s32[8]{0:T(128)S(1)} %fusion.27), kind=kOutput, calls=%fused_computation.9 | convolution fusion | flops 67372032 | bytes 8912928 | tf_op jit(solution)/shard_map/ks,srd->krd/dot_general | solution.py:17
  314.1 83.5 %all-gather.9.cloned.1.call-done = f32[16,384,128]{2,1,0:T(8,128)} async-done(((f32[1,384,128]{2,1,0:T(8,128)}), f32[16,384,128]{2,1,0:T(8,128)}) %all-gather.9.cloned.1.call-update) | async-done | bytes 3145744 | tf_op jit(solution)/shard_map/all_gather | solution.py:59
  397.7 2.0 reduce_sum.39
  399.7 0.1 convert_element_type.27
  399.8 0.1 copy.22
  400.0 0.6 fusion.13
  400.6 12.8 %fusion.5 = bf16[768,512]{1,0:T(8,128)(2,1)} fusion(f32[768,512,1]{1,0,2:T(8,128)S(1)} %fusion.13, bf16[768,8192]{1,0:T(8,128)(2,1)} %all-gather.5.cloned.1.call-done, bf16[8192,512]{1,0:T(8,128)(2,1)} %param.8), kind=kOutput, calls=%fused_computation.6 | convolution fusion | flops 6443630592 | bytes 23330816 | tf_op jit(solution)/shard_map/dot_general | solution.py:44
  (8 shorter events, 0.1 us)
Async XLA Ops:
  6.5 3.0 copy-start
  6.5 60.1 %all-gather.7.cloned.1.call-start = ((), (), s32[]{:S(2)}) async-start(), calls=%async_computation.1 | async-start | bytes 8912896 | tf_op jit(solution)/shard_map/all_gather | solution.py:34
  7.3 241.4 %all-gather.5.cloned.1.call-start = ((), (), s32[]{:S(2)}) async-start(), calls=%async_computation | async-start | bytes 13369344 | tf_op jit(solution)/shard_map/all_gather | solution.py:43
  8.0 293.8 %all-gather.11.cloned.1.call-start = ((), (), s32[]{:S(2)}) async-start(), calls=%async_computation.3 | async-start | bytes 8912896 | tf_op jit(solution)/shard_map/all_gather | solution.py:35
  8.7 388.9 %all-gather.9.cloned.1.call-start = ((), (), s32[]{:S(2)}) async-start(), calls=%async_computation.2 | async-start | bytes 3342336 | tf_op jit(solution)/shard_map/all_gather | solution.py:59
Sparse Core Ops, SparseCore 0:
  9.2 57.4 all-gather.6
  69.2 179.3 all-gather.4
  250.5 51.2 all-gather.10
  304.2 93.3 all-gather.8
